TPU v7x, 32 devices: a whole 2x2x4 slice. The times are simulated.
32 devices in a mesh: groups: 2 (over y), ctx: 4 (over z), head: 2 (over x), rep: 2 (over core).
Axes of the slice: x: 2, y: 2, z: 4, core: 2. Of those that a mesh axis runs over, the one named last changes fastest.
Arguments:
- query: bfloat16 [2048, 4096], P(('groups', 'ctx', 'rep'), 'head'), parts along dimension 0, may hold values from -23.069359 to 23.069359
- key: bfloat16 [4096, 1024], P(('groups', 'ctx'), 'head'), parts along dimension 0, may hold values from -6 to 6
- value: bfloat16 [4096, 1024], P(('groups', 'ctx'), 'head'), parts along dimension 0, may hold values from -24 to 24
- out_weight: bfloat16 [4096, 4096], P('head'), may hold values from -0.375 to 0.375
- cotangent: bfloat16 [2048, 4096], P(('groups', 'ctx', 'rep')), parts along dimension 0, may hold values from -6 to 6
- response: int32 [2048], P(('groups', 'ctx', 'rep')), parts along dimension 0, may hold values 0 or 1
- segment_ids: int32 [4096], P(('groups', 'ctx')), parts along dimension 0, may hold values from 0 to 31, never falling along the last dimension, each value on 1 to 128 neighbouring positions
- masked_segments: int32 [8], P('groups'), parts along dimension 0, may hold values from 0 to 31
Outputs:
- patch_effect: bfloat16 [2048, 4096], P(('groups', 'ctx', 'rep'), 'head'), parts along dimension 0
- token_attr: float32 [4096], P(('groups', 'ctx')), parts along dimension 0
- segment_attr: float32 [64], P('groups'), parts along dimension 0
There are 2 independent parts, one for each index of `groups`. A program takes and returns all parts, laid end to end along the dimension named above; an argument that names none is the same for every part. Nothing has to cross between parts.
All inputs are finite; a program needn't handle non-finite values. No bound on the sum of `response` on one device may be relied on, other than what follows from the above.
Results may differ from a plain program's by a relative error of at most 0.0095.
Values may be sent and summed in bfloat16 or wider, within the bound.
No kernel may reach another device: no remote copies, remote signals or barrier semaphores. Data moves between devices by JAX's collectives and lax.ppermute only.
A program may use at most 128 MiB of HBM per device.

v0:
```python
from functools import partial
import jax
import jax.numpy as jnp
from jax import lax
from jax.sharding import PartitionSpec as P

HD = 128
SEG_DEV = 8
NEG_FILL = -1e30


def split_heads(incoming):
    return incoming.reshape(incoming.shape[0], -1, HD)


def block_scores(query_rows, key_block):
    raw_scores = jnp.einsum(
        "gqd,tgd->gqt", query_rows, split_heads(key_block), preferred_element_type=jnp.float32
    )
    return raw_scores * HD ** (-0.5)


def visible_keys(row_pos, first_key, key_rows):
    key_pos = first_key + jnp.arange(key_rows, dtype=jnp.int32)
    return key_pos[None, None, :] <= row_pos[None, :, None]


def online_update(running, scores, allowed, value_heads):
    row_top, row_total, weighted = running
    chosen = jnp.where(allowed, scores, NEG_FILL)
    new_top = jnp.maximum(row_top, jnp.max(chosen, axis=2))
    shrink = jnp.exp(row_top - new_top)
    weights = jnp.where(allowed, jnp.exp(chosen - new_top[:, :, None]), 0.0)
    row_total = row_total * shrink + jnp.sum(weights, axis=2)
    weighted = weighted * shrink[:, :, None] + jnp.einsum(
        "gqt,tgd->gqd",
        weights.astype(jnp.bfloat16),
        value_heads,
        preferred_element_type=jnp.float32,
    )
    return (new_top, row_total, weighted)


def forward_piece(query_rows, row_pos, running, incoming, first_key):
    key_block, value_block, kept_flag = incoming
    scores = block_scores(query_rows, key_block)
    visible = visible_keys(row_pos, first_key, key_block.shape[0])
    kept_visible = jnp.logical_and(visible, kept_flag[None, None, :] > 0)
    value_heads = split_heads(value_block)
    return (
        online_update(running[0], scores, visible, value_heads),
        online_update(running[1], scores, kept_visible, value_heads),
    )


def backward_terms(
    query_rows, row_pos, grad_rows, log_total, row_dot, key_block, value_block, first_key
):
    scores = block_scores(query_rows, key_block)
    visible = visible_keys(row_pos, first_key, key_block.shape[0])
    shifted = jnp.where(visible, scores - log_total[:, :, None], 0.0)
    probability = jnp.where(visible, jnp.exp(shifted), 0.0)
    grad_prob = jnp.einsum(
        "gqd,tgd->gqt", grad_rows, split_heads(value_block), preferred_element_type=jnp.float32
    )
    return jnp.sum(
        probability * (grad_prob + (grad_prob - row_dot[:, :, None]) * shifted), axis=(0, 1)
    )


def blockwise(stepper, state_in, incoming, block_rows):
    length = jax.tree.leaves(incoming)[0].shape[0]

    def advance(counter, state_now):
        offset = counter * block_rows
        portion = jax.tree.map(
            lambda member: lax.dynamic_slice_in_dim(member, offset, block_rows, 0), incoming
        )
        return stepper(state_now, portion, offset)

    return lax.fori_loop(0, length // block_rows, advance, state_in)


def finish_pass(running):
    row_top, row_total, weighted = running
    return (weighted / row_total[:, :, None], row_top + jnp.log(row_total))


def local(query, key, value, out_weight, cotangent, response, segment_ids, masked_segments):
    ctx_count = lax.axis_size("ctx")
    rep_count = lax.axis_size("rep")
    ctx_at = lax.axis_index("ctx")
    rep_at = lax.axis_index("rep")
    query_count = query.shape[0]
    key_count = key.shape[0]
    kv_local = key.shape[1] // HD
    heads_local = query.shape[1] // HD
    group_size = heads_local // kv_local
    context_len = key_count * ctx_count
    query_base = context_len - query_count * ctx_count * rep_count
    row_width = group_size * query_count
    kept_flag = jnp.where(
        jnp.any(segment_ids[:, None] == masked_segments[None, :], axis=1), 0.0, 1.0
    ).astype(jnp.bfloat16)
    grad_masked = jnp.where(response[:, None] > 0, cotangent, jnp.zeros_like(cotangent))
    grad_out = jnp.dot(grad_masked, out_weight.T, preferred_element_type=jnp.float32).astype(
        jnp.bfloat16
    )

    def grouped(rows_in):
        return rows_in.reshape(query_count, kv_local, group_size, HD).transpose(1, 2, 0, 3)

    fresh_state = (
        jnp.full((kv_local, row_width), NEG_FILL, jnp.float32),
        jnp.zeros((kv_local, row_width), jnp.float32),
        jnp.zeros((kv_local, row_width, HD), jnp.float32),
    )
    starting = (fresh_state, fresh_state)
    query_rows = grouped(query).reshape(kv_local, row_width, HD)
    grad_own = grouped(grad_out).reshape(kv_local, row_width, HD)
    base_pos = (
        query_base
        + (ctx_at * rep_count + rep_at) * query_count
        + jnp.arange(query_count, dtype=jnp.int32)
    )
    own_pos = jnp.tile(base_pos, group_size)
    forward_step = partial(forward_piece, query_rows, own_pos)
    running = blockwise(
        forward_step,
        starting,
        (
            lax.all_gather(key, "ctx", axis=0, tiled=True),
            lax.all_gather(value, "ctx", axis=0, tiled=True),
            lax.all_gather(kept_flag, "ctx", axis=0, tiled=True),
        ),
        key_count,
    )
    clean_out, log_total = finish_pass(running[0])
    masked_out, _ = finish_pass(running[1])
    row_dot = jnp.sum(grad_own.astype(jnp.float32) * clean_out, axis=2)

    def backward_step(total_now, incoming, first_key):
        added = backward_terms(
            query_rows, own_pos, grad_own, log_total, row_dot, incoming[0], incoming[1], first_key
        )
        current = lax.dynamic_slice_in_dim(total_now, first_key, incoming[0].shape[0], 0)
        return lax.dynamic_update_slice_in_dim(total_now, current + added, first_key, 0)

    empty_attr = jnp.zeros((context_len,), jnp.float32)
    attr_all = blockwise(
        backward_step,
        empty_attr,
        (
            lax.all_gather(key, "ctx", axis=0, tiled=True),
            lax.all_gather(value, "ctx", axis=0, tiled=True),
        ),
        key_count,
    )
    local_attr = lax.psum_scatter(attr_all, "ctx", scatter_dimension=0, tiled=True)
    change = (
        (masked_out - clean_out)
        .reshape(kv_local, group_size, query_count, HD)
        .transpose(2, 0, 1, 3)
        .reshape(query_count, heads_local * HD)
        .astype(jnp.bfloat16)
    )
    projected = jnp.dot(change, out_weight, preferred_element_type=jnp.float32)
    patch_effect = lax.psum_scatter(projected, "head", scatter_dimension=1, tiled=True).astype(
        jnp.bfloat16
    )
    token_attr = lax.psum(local_attr, ("head", "rep"))
    onehot = (
        segment_ids[:, None] == jnp.arange(SEG_DEV * ctx_count, dtype=jnp.int32)[None, :]
    ).astype(jnp.float32)
    segment_attr = lax.psum(jnp.dot(token_attr, onehot, precision=lax.Precision.HIGHEST), "ctx")
    return (patch_effect, token_attr, segment_attr)


def solution(mesh):
    return jax.shard_map(
        local,
        mesh=mesh,
        in_specs=(
            P(("groups", "ctx", "rep"), "head"),
            P(("groups", "ctx"), "head"),
            P(("groups", "ctx"), "head"),
            P("head", None),
            P(("groups", "ctx", "rep"), None),
            P(("groups", "ctx", "rep")),
            P(("groups", "ctx")),
            P("groups"),
        ),
        out_specs=(P(("groups", "ctx", "rep"), "head"), P(("groups", "ctx")), P("groups")),
        check_vma=False,
    )
```

profile of v0, /device:TPU:0, one launch (start us, length us, event | category | flops | bytes accessed | tf_op | source)
XLA Modules:
  0.0 224.0 jit_solution(5980120812336782876)
XLA Ops:
  7.3 2.1 copy.57
  9.5 2.0 copy.59
  11.6 1.4 reshape.201
  13.3 13.7 %all-gather = bf16[4,1,512]{2,1,0:T(2,128)(2,1)S(1)} all-gather(bf16[1,1,512]{2,1,0:T(2,128)(2,1)S(1)} %reshape.205), channel_id=1, replica_groups=mesh['groups'=2,'ctx'=4,'head'=2,'rep'=2] {'ctx'}, dimensions={0}, use_global_device_ids=true | all-gather | bytes 5120 | tf_op jit(solution)/shard_map/all_gather | solution.py:134
  27.1 11.5 %convolution_convert_fusion = bf16[128,2048]{1,0:T(8,128)(2,1)S(1)} fusion(bf16[2048,4096]{1,0:T(8,128)(2,1)} %param.15, bf16[128,4096]{1,0:T(8,128)(2,1)S(1)} %copy-done.3, pred[128]{0:T(512)(128)(4,1)S(1)} %broadcast_compare_fusion.2), kind=kOutput, calls=%fused_computation.53 | convolution fusion | flops 2148270080 | bytes 18350208 | tf_op jit(solution)/shard_map/dot_general | solution.py:106
  40.5 18.3 %all-gather.4.cloned.1.call-done = bf16[2048,512]{0,1:T(8,128)(2,1)} async-done(((bf16[512,512]{0,1:T(8,128)(2,1)}), bf16[2048,512]{0,1:T(8,128)(2,1)}) %all-gather.4.cloned.1.call-update) | async-done | bytes 2097168 | tf_op jit(solution)/shard_map/all_gather | solution.py:132
  58.9 46.4 %all-gather.6.cloned.1.call-done = bf16[2048,512]{0,1:T(8,128)(2,1)} async-done(((bf16[512,512]{0,1:T(8,128)(2,1)}), bf16[2048,512]{0,1:T(8,128)(2,1)}) %all-gather.6.cloned.1.call-update) | async-done | bytes 2097168 | tf_op jit(solution)/shard_map/all_gather | solution.py:133
  105.2 54.5 %while.39 = (s32[]{:T(128)}, f32[4,512]{1,0:T(4,128)S(1)}, f32[4,512]{1,0:T(4,128)S(1)}, f32[4,512,128]{2,1,0:T(8,128)S(1)}, f32[4,512]{1,0:T(4,128)S(1)}, /*ind...) while((s32[]{:T(128)}, f32[4,512]{1,0:T(4,128)S(1)}, ...), condition=%wide.region_6.7_spmd.clone, body=%wide.region_1.6_spmd.clone.sunk | while | flops 832591872 | bytes 52702004 | solution.py:81
  105.6 1.1 constant_dynamic-slice_fusion.8
  106.7 3.4 %fusion.81 = (f32[4,512]{1,0:T(4,128)S(1)}, f32[4,512]{1,0:T(4,128)S(1)}, f32[4,512,512]{2,1,0:T(8,128)}) fusion(pred[512,512]{0,1:T(8,128)(4,1)S(1)} %get-tuple-element.631, pred[512,512]{0,1:T(8,128)(4,1)S(1)} %get-tuple-element.632, bf16[512,4,128]{0,2,1:T(8,128)(2,1)S(1)} %bitcast.121, bf16[4,512,128]{2,1,0:T(8,128)(2,1)S(1)} %get-tuple-element.682), kind=kOutput, calls=%fused_computation.19.clone.1 | convolution fusion | flops 273674240 | bytes 5783552 | tf_op jit(solution)/shard_map/while/body/eval_jaxpr/gqd,tgd->gqt/dot_general | solution.py:17
  110.1 3.7 %fusion.82 = (f32[4,512]{1,0:T(4,128)S(1)}, f32[4,512]{1,0:T(4,128)S(1)}) fusion(f32[4,512,512]{2,1,0:T(8,128)} %get-tuple-element.634, f32[4,512]{1,0:T(4,128)S(1)} %select_maximum_fusion.5, pred[512,512]{0,1:T(8,128)(4,1)S(1)} %get-tuple-element.631, f32[4,512]{1,0:T(4,128)S(1)} %select_maximum_fusion.4, pred[512,512]{0,1:T(8,128)(4,1)S(1)} %get-tuple-element.632), kind=kLoop, calls=%fused_computation.23.clone.1 | loop fusion | flops 9433088 | bytes 4751360 | tf_op jit(solution)/shard_map/while/body/eval_jaxpr/reduce_sum | solution.py:34
  113.9 1.1 constant_dynamic-slice_fusion.9
  115.0 1.9 fusion.85
  116.9 1.9 fusion.84
  119.3 1.1 constant_dynamic-slice_fusion.8
  120.4 3.4 %fusion.81 = (f32[4,512]{1,0:T(4,128)S(1)}, f32[4,512]{1,0:T(4,128)S(1)}, f32[4,512,512]{2,1,0:T(8,128)}) fusion(pred[512,512]{0,1:T(8,128)(4,1)S(1)} %get-tuple-element.631, pred[512,512]{0,1:T(8,128)(4,1)S(1)} %get-tuple-element.632, bf16[512,4,128]{0,2,1:T(8,128)(2,1)S(1)} %bitcast.121, bf16[4,512,128]{2,1,0:T(8,128)(2,1)S(1)} %get-tuple-element.682), kind=kOutput, calls=%fused_computation.19.clone.1 | convolution fusion | flops 273674240 | bytes 5783552 | tf_op jit(solution)/shard_map/while/body/eval_jaxpr/gqd,tgd->gqt/dot_general | solution.py:17
  123.8 3.7 %fusion.82 = (f32[4,512]{1,0:T(4,128)S(1)}, f32[4,512]{1,0:T(4,128)S(1)}) fusion(f32[4,512,512]{2,1,0:T(8,128)} %get-tuple-element.634, f32[4,512]{1,0:T(4,128)S(1)} %select_maximum_fusion.5, pred[512,512]{0,1:T(8,128)(4,1)S(1)} %get-tuple-element.631, f32[4,512]{1,0:T(4,128)S(1)} %select_maximum_fusion.4, pred[512,512]{0,1:T(8,128)(4,1)S(1)} %get-tuple-element.632), kind=kLoop, calls=%fused_computation.23.clone.1 | loop fusion | flops 9433088 | bytes 4751360 | tf_op jit(solution)/shard_map/while/body/eval_jaxpr/reduce_sum | solution.py:34
  127.5 1.1 constant_dynamic-slice_fusion.9
  128.6 1.9 fusion.85
  130.6 1.9 fusion.84
  132.9 1.1 constant_dynamic-slice_fusion.8
  134.0 3.4 %fusion.81 = (f32[4,512]{1,0:T(4,128)S(1)}, f32[4,512]{1,0:T(4,128)S(1)}, f32[4,512,512]{2,1,0:T(8,128)}) fusion(pred[512,512]{0,1:T(8,128)(4,1)S(1)} %get-tuple-element.631, pred[512,512]{0,1:T(8,128)(4,1)S(1)} %get-tuple-element.632, bf16[512,4,128]{0,2,1:T(8,128)(2,1)S(1)} %bitcast.121, bf16[4,512,128]{2,1,0:T(8,128)(2,1)S(1)} %get-tuple-element.682), kind=kOutput, calls=%fused_computation.19.clone.1 | convolution fusion | flops 273674240 | bytes 5783552 | tf_op jit(solution)/shard_map/while/body/eval_jaxpr/gqd,tgd->gqt/dot_general | solution.py:17
  137.4 3.7 %fusion.82 = (f32[4,512]{1,0:T(4,128)S(1)}, f32[4,512]{1,0:T(4,128)S(1)}) fusion(f32[4,512,512]{2,1,0:T(8,128)} %get-tuple-element.634, f32[4,512]{1,0:T(4,128)S(1)} %select_maximum_fusion.5, pred[512,512]{0,1:T(8,128)(4,1)S(1)} %get-tuple-element.631, f32[4,512]{1,0:T(4,128)S(1)} %select_maximum_fusion.4, pred[512,512]{0,1:T(8,128)(4,1)S(1)} %get-tuple-element.632), kind=kLoop, calls=%fused_computation.23.clone.1 | loop fusion | flops 9433088 | bytes 4751360 | tf_op jit(solution)/shard_map/while/body/eval_jaxpr/reduce_sum | solution.py:34
  141.2 1.1 constant_dynamic-slice_fusion.9
  142.3 1.9 fusion.85
  144.2 1.9 fusion.84
  146.6 1.1 constant_dynamic-slice_fusion.8
  147.7 3.4 %fusion.81 = (f32[4,512]{1,0:T(4,128)S(1)}, f32[4,512]{1,0:T(4,128)S(1)}, f32[4,512,512]{2,1,0:T(8,128)}) fusion(pred[512,512]{0,1:T(8,128)(4,1)S(1)} %get-tuple-element.631, pred[512,512]{0,1:T(8,128)(4,1)S(1)} %get-tuple-element.632, bf16[512,4,128]{0,2,1:T(8,128)(2,1)S(1)} %bitcast.121, bf16[4,512,128]{2,1,0:T(8,128)(2,1)S(1)} %get-tuple-element.682), kind=kOutput, calls=%fused_computation.19.clone.1 | convolution fusion | flops 273674240 | bytes 5783552 | tf_op jit(solution)/shard_map/while/body/eval_jaxpr/gqd,tgd->gqt/dot_general | solution.py:17
  151.1 3.7 %fusion.82 = (f32[4,512]{1,0:T(4,128)S(1)}, f32[4,512]{1,0:T(4,128)S(1)}) fusion(f32[4,512,512]{2,1,0:T(8,128)} %get-tuple-element.634, f32[4,512]{1,0:T(4,128)S(1)} %select_maximum_fusion.5, pred[512,512]{0,1:T(8,128)(4,1)S(1)} %get-tuple-element.631, f32[4,512]{1,0:T(4,128)S(1)} %select_maximum_fusion.4, pred[512,512]{0,1:T(8,128)(4,1)S(1)} %get-tuple-element.632), kind=kLoop, calls=%fused_computation.23.clone.1 | loop fusion | flops 9433088 | bytes 4751360 | tf_op jit(solution)/shard_map/while/body/eval_jaxpr/reduce_sum | solution.py:34
  154.8 1.1 constant_dynamic-slice_fusion.9
  155.9 1.9 fusion.85
  157.8 1.9 fusion.84
  159.8 2.1 multiply_reduce_fusion
  162.2 9.5 %fusion.39 = f32[128,4096]{1,0:T(8,128)} fusion(bf16[128,2048]{0,1:T(8,128)(2,1)S(1)} %bitcast.122, bf16[2048,4096]{1,0:T(8,128)(2,1)} %param.15), kind=kOutput, calls=%fused_computation.70 | convolution fusion | flops 2147483648 | bytes 19398656 | tf_op jit(solution)/shard_map/dot_general | solution.py:167
  171.8 18.3 %while.38 = (s32[]{:T(128)}, f32[2048]{0:T(1024)S(1)}, bf16[2048,512]{0,1:T(8,128)(2,1)}, bf16[4,512,128]{2,1,0:T(8,128)(2,1)S(1)}, f32[4,512]{1,0:T(4,128)S(1)}...) while((s32[]{:T(128)}, f32[2048]{0:T(1024)S(1)}, ...), condition=%wide.region_11.12_spmd.clone, body=%wide.region_9.11_spmd.clone.sunk | while | flops 546570752 | bytes 13140663 | solution.py:81
  171.8 1.3 constant_dynamic-slice_fusion.7
  173.1 0.7 fusion.73
  174.0 2.1 fusion.74
  176.3 1.5 constant_dynamic-slice_fusion.7
  178.7 2.1 fusion.74
  181.0 1.3 constant_dynamic-slice_fusion.7
  183.2 2.1 fusion.74
  185.5 1.3 constant_dynamic-slice_fusion.7
  187.7 2.1 fusion.74
  190.0 9.4 %all-reduce = f32[2048]{0:T(1024)S(1)} all-reduce(f32[2048]{0:T(1024)S(1)} %get-tuple-element.365), channel_id=3, replica_groups=mesh['groups'=2,'ctx'=4,'head'=2,'rep'=2] {'ctx'}, use_global_device_ids=true, to_apply=%region_12.13.clone | all-reduce | flops 2048 | bytes 16384
  199.5 5.6 %psum.14 = f32[512]{0:T(512)S(1)} all-reduce(f32[512]{0:T(512)S(1)} %dynamic-slice.1), channel_id=1, replica_groups=mesh['groups'=2,'ctx'=4,'head'=2,'rep'=2] {'head','rep'}, use_global_device_ids=true, to_apply=%region_13.14 | all-reduce | flops 512 | bytes 4096 | tf_op jit(solution)/shard_map/psum | solution.py:171
  205.4 10.0 %psum.15 = f32[32]{0:T(128)} all-reduce(f32[32]{0:T(128)S(1)} %convolution_bitcast_fusion), channel_id=1, replica_groups=mesh['groups'=2,'ctx'=4,'head'=2,'rep'=2] {'ctx'}, use_global_device_ids=true, to_apply=%region_14.15 | all-reduce | flops 32 | bytes 256 | tf_op jit(solution)/shard_map/psum | solution.py:175
  215.4 2.1 convert_element_type.44
  (120 shorter events, 7.9 us)
Async XLA Ops:
  7.2 6.0 %copy-start.4 = (s32[512]{0:T(512)S(1)}, s32[512]{0:T(512)}, u32[]{:S(2)}) copy-start(s32[512]{0:T(512)} %param.18) | copy-start | bytes 6148
  7.2 6.0 %copy-start.6 = (s32[4]{0:T(128)S(1)}, s32[4]{0:T(128)}, u32[]{:S(2)}) copy-start(s32[4]{0:T(128)} %param.19) | copy-start | bytes 52
  7.2 19.9 %copy-start.7 = (s32[128]{0:T(128)S(1)}, s32[128]{0:T(128)}, u32[]{:S(2)}) copy-start(s32[128]{0:T(128)} %param.17) | copy-start | bytes 1540
  7.2 19.9 %copy-start.3 = (bf16[128,4096]{1,0:T(8,128)(2,1)S(1)}, bf16[128,4096]{1,0:T(8,128)(2,1)}, u32[]{:S(2)}) copy-start(bf16[128,4096]{1,0:T(8,128)(2,1)} %param.16) | copy-start | bytes 3145732
  7.2 51.7 %all-gather.4.cloned.1.call-start = ((), (), s32[]{:S(2)}) async-start(), calls=%async_computation.1 | async-start | bytes 2621440 | tf_op jit(solution)/shard_map/all_gather | solution.py:132
  9.4 95.8 %all-gather.6.cloned.1.call-start = ((), (), s32[]{:S(2)}) async-start(), calls=%async_computation.2 | async-start | bytes 2621440 | tf_op jit(solution)/shard_map/all_gather | solution.py:133
  11.5 203.9 %reduce-scatter.2.cloned.1.call-start = ((), (), s32[]{:S(2)}) async-start(), calls=%async_computation.3 | async-start | bytes 3145728 | tf_op jit(solution)/shard_map/reduce_scatter | solution.py:168
  27.1 12.1 %copy-start.8 = (u32[32]{0:T(128)S(1)}, u32[32]{0:T(128)}, u32[]{:S(2)}) copy-start(u32[32]{0:T(128)} %constant.131) | copy-start | bytes 388
  110.1 4.9 %copy-start = (f32[4,512,512]{2,1,0:T(8,128)S(1)}, f32[4,512,512]{2,1,0:T(8,128)}, u32[]{:S(2)}) copy-start(f32[4,512,512]{2,1,0:T(8,128)} %get-tuple-element.634) | copy-start | bytes 12582916 | tf_op jit(solution)/shard_map/while
  110.1 4.9 %copy-start.1 = (f32[4,512,128]{2,1,0:T(8,128)S(1)}, f32[4,512,128]{2,1,0:T(8,128)}, u32[]{:S(2)}) copy-start(f32[4,512,128]{2,1,0:T(8,128)} %get-tuple-element.664) | copy-start | bytes 3145732 | tf_op jit(solution)/shard_map/while
  116.9 1.9 copy-start.2
  123.8 4.9 %copy-start = (f32[4,512,512]{2,1,0:T(8,128)S(1)}, f32[4,512,512]{2,1,0:T(8,128)}, u32[]{:S(2)}) copy-start(f32[4,512,512]{2,1,0:T(8,128)} %get-tuple-element.634) | copy-start | bytes 12582916 | tf_op jit(solution)/shard_map/while
  123.8 4.9 %copy-start.1 = (f32[4,512,128]{2,1,0:T(8,128)S(1)}, f32[4,512,128]{2,1,0:T(8,128)}, u32[]{:S(2)}) copy-start(f32[4,512,128]{2,1,0:T(8,128)} %get-tuple-element.664) | copy-start | bytes 3145732 | tf_op jit(solution)/shard_map/while
  130.6 1.9 copy-start.2
  137.4 4.9 %copy-start = (f32[4,512,512]{2,1,0:T(8,128)S(1)}, f32[4,512,512]{2,1,0:T(8,128)}, u32[]{:S(2)}) copy-start(f32[4,512,512]{2,1,0:T(8,128)} %get-tuple-element.634) | copy-start | bytes 12582916 | tf_op jit(solution)/shard_map/while
  137.4 4.9 %copy-start.1 = (f32[4,512,128]{2,1,0:T(8,128)S(1)}, f32[4,512,128]{2,1,0:T(8,128)}, u32[]{:S(2)}) copy-start(f32[4,512,128]{2,1,0:T(8,128)} %get-tuple-element.664) | copy-start | bytes 3145732 | tf_op jit(solution)/shard_map/while
  144.2 1.9 copy-start.2
  151.0 4.9 %copy-start = (f32[4,512,512]{2,1,0:T(8,128)S(1)}, f32[4,512,512]{2,1,0:T(8,128)}, u32[]{:S(2)}) copy-start(f32[4,512,512]{2,1,0:T(8,128)} %get-tuple-element.634) | copy-start | bytes 12582916 | tf_op jit(solution)/shard_map/while
  151.0 4.9 %copy-start.1 = (f32[4,512,128]{2,1,0:T(8,128)S(1)}, f32[4,512,128]{2,1,0:T(8,128)}, u32[]{:S(2)}) copy-start(f32[4,512,128]{2,1,0:T(8,128)} %get-tuple-element.664) | copy-start | bytes 3145732 | tf_op jit(solution)/shard_map/while
  157.8 1.9 copy-start.2
  205.1 12.4 %copy-start.5 = (f32[512]{0:T(512)}, f32[512]{0:T(512)S(1)}, u32[]{:S(2)}) copy-start(f32[512]{0:T(512)S(1)} %psum.14) | copy-start | bytes 6148
Sparse Core Ops, SparseCore 0:
  10.2 48.6 all-gather.3
  60.4 44.7 all-gather.5
  171.9 30.5 reduce-scatter.1
where the time goes:
time: 225 us; the launch traced here: 224 us
  waiting for transfers between devices  64.7 us (29%)
  matrix products  61.2 us (27%)
  blocking collectives  38.7 us (17%)
  other arithmetic  22.6 us (10%)
  local copies, waits for them, and re-layouts  21.4 us (10%)
  between operations  14.7 us (7%)
    all_gather x1, waiting for transfers between devices, local(): lax.all_gather(value, 'ctx', axis=0, tiled=True)  46.4 us
    all_gather x1, waiting for transfers between devices, local(): lax.all_gather(key, 'ctx', axis=0, tiled=True)  18.3 us
    dot_general x8, matrix products, block_scores(): jnp.einsum('gqd,tgd->gqt', query_rows, split_heads(key_block), preferred_...  16.3 us
    dot_general x8, matrix products, online_update(): jnp.einsum('gqt,tgd->gqd', weights.astype(jnp.bfloat16), value_heads, pre...  15.3 us
    reduce_sum x4, other arithmetic, online_update(): row_total = row_total * shrink + jnp.sum(weights, axis=2)  14.8 us
    dynamic_slice x12, local copies, waits for them, and re-layouts, advance(): lax.dynamic_slice_in_dim(member, offset, block_rows, 0)  14 us
    all_gather x1, blocking collectives, local(): lax.all_gather(kept_flag, 'ctx', axis=0, tiled=True)  13.7 us
    dot_general x1, matrix products, local(): jnp.dot(grad_masked, out_weight.T, preferred_element_type=jnp.float32)  11.5 us
  transfers between devices with their start and end apart: 3, of which 2 were waited for; matrix products, arithmetic and copies ran while one was open for 16% of the time, Pallas kernels for 0%

commit v1 on v0

--- a/solution.py
+++ b/solution.py
@@ -7,6 +7,17 @@
 HD = 128
 SEG_DEV = 8
 NEG_FILL = -1e30
+
+
+def ring_gather(x, axis, dim):
+    ways = lax.axis_size(axis)
+    pieces = [x]
+    for far in range(1, ways):
+        pieces.append(
+            lax.ppermute(pieces[far - 1], axis, [(d, (d - 1) % ways) for d in range(ways)])
+        )
+    line = jnp.concatenate(pieces, axis=dim)
+    return jnp.roll(line, lax.axis_index(axis) * x.shape[dim], axis=dim)
 
 
 def split_heads(incoming):
@@ -129,7 +140,7 @@
         forward_step,
         starting,
         (
-            lax.all_gather(key, "ctx", axis=0, tiled=True),
+            ring_gather(key, "ctx", 0),
             lax.all_gather(value, "ctx", axis=0, tiled=True),
             lax.all_gather(kept_flag, "ctx", axis=0, tiled=True),
         ),

time: 225 us -> 216 us (0.960)
  waiting for transfers between devices: 64.7 us -> 37.7 us
  starting transfers between devices: 0.12 us -> 9.56 us
  blocking collectives: 38.7 us -> 45.1 us
    all_gather x1, waiting for transfers between devices: 46.4 us -> 0.02 us  [local(): lax.all_gather(value, 'ctx', axis=0, tiled=True)]
    ppermute x0 -> x3, waiting for transfers between devices: none -> 37.6 us  [ring_gather(): lax.ppermute(pieces[far - 1], axis, [(d, (d - 1) % ways) for d in range(w...]
    all_gather x1, waiting for transfers between devices: 18.3 us -> 0.02 us  [local(): lax.all_gather(key, 'ctx', axis=0, tiled=True)]
    ppermute x0 -> x3, starting transfers between devices: none -> 9.44 us  [ring_gather(): lax.ppermute(pieces[far - 1], axis, [(d, (d - 1) % ways) for d in range(w...]
    all_gather x1, blocking collectives: 13.7 us -> 18.9 us  [local(): lax.all_gather(kept_flag, 'ctx', axis=0, tiled=True)]
    dynamic_slice x12, local copies, waits for them, and re-layouts: 14 us -> 9.61 us  [advance(): lax.dynamic_slice_in_dim(member, offset, block_rows, 0)]
    while x32 -> x48, local copies, waits for them, and re-layouts: 0.07 us -> 4.28 us
    unnamed x18 -> x29, local copies, waits for them, and re-layouts: 4.96 us -> 4.57 us
  transfers between devices with their start and end apart: 3 -> 6, of which waited for: 2 -> 2; matrix products, arithmetic and copies ran while one was open for 16% -> 46% of each run, Pallas kernels for 0% -> 0%
where the time goes in v1:
time: 216 us
  matrix products  62.5 us (29%)
  blocking collectives  45.1 us (21%)
  waiting for transfers between devices  37.7 us (17%)
  other arithmetic  23.4 us (11%)
  local copies, waits for them, and re-layouts  21.8 us (10%)
  between operations  14.8 us (7%)
  starting transfers between devices  9.56 us (4%)
    ppermute x3, waiting for transfers between devices, ring_gather(): lax.ppermute(pieces[far - 1], axis, [(d, (d - 1) % ways) for d in range(w...  37.6 us
    all_gather x1, blocking collectives, local(): lax.all_gather(kept_flag, 'ctx', axis=0, tiled=True)  18.9 us
    dot_general x8, matrix products, block_scores(): jnp.einsum('gqd,tgd->gqt', query_rows, split_heads(key_block), preferred_...  16.3 us
    dot_general x8, matrix products, online_update(): jnp.einsum('gqt,tgd->gqd', weights.astype(jnp.bfloat16), value_heads, pre...  15.3 us
    reduce_sum x4, other arithmetic, online_update(): row_total = row_total * shrink + jnp.sum(weights, axis=2)  14.8 us
    dot_general x1, matrix products, local(): jnp.dot(grad_masked, out_weight.T, preferred_element_type=jnp.float32)  12.7 us
    unnamed x1, blocking collectives  11.5 us
    dynamic_slice x12, local copies, waits for them, and re-layouts, advance(): lax.dynamic_slice_in_dim(member, offset, block_rows, 0)  9.61 us
  transfers between devices with their start and end apart: 6, of which 2 were waited for; matrix products, arithmetic and copies ran while one was open for 46% of the time, Pallas kernels for 0%

profile of v1, /device:TPU:0, one launch (start us, length us, event | category | flops | bytes accessed | tf_op | source)
XLA Modules:
  0.0 215.6 jit_solution(11295653107064876547)
XLA Ops:
  7.2 2.0 copy.70
  9.3 1.3 copy.67
  10.6 5.1 %collective-permute-start = (bf16[512,512]{0,1:T(8,128)(2,1)S(1)}, bf16[512,512]{0,1:T(8,128)(2,1)S(1)}, u32[]{:S(2)}, u32[]{:S(2)}) collective-permute-start(bf16[512,512]{0,1:T(8,128)(2,1)S(1)} %copy.67), channel_id=1, source_target_pairs={{0,12},{4,0},{8,4},{12,8},{1,13},{5,1},{9,5},{13,9},{2,14},{6,2},{... | collective-permute-start | bytes 1572872 | tf_op jit(solution)/shard_map/ppermute | solution.py:17
  16.4 17.8 %collective-permute-done = bf16[512,512]{0,1:T(8,128)(2,1)S(1)} collective-permute-done((bf16[512,512]{0,1:T(8,128)(2,1)S(1)}, bf16[512,512]{0,1:T(8,128)(2,1)S(1)}, u32[]{:S(2)}, u32[]{:S(2)}) %collective-permute-start) | collective-permute-done | bytes 524320 | tf_op jit(solution)/shard_map/ppermute | solution.py:17
  34.3 4.3 %collective-permute-start.1 = (bf16[512,512]{0,1:T(8,128)(2,1)S(1)}, bf16[512,512]{0,1:T(8,128)(2,1)S(1)}, u32[]{:S(2)}, u32[]{:S(2)}) collective-permute-start(bf16[512,512]{0,1:T(8,128)(2,1)S(1)} %collective-permute-done), channel_id=1, source_target_pairs={{0,12},{4,0},{8,4},{12,8},{1,13},{5,1},{9,5},{13,9},{2,14},{6,2},{... | collective-permute-start | bytes 1572872 | tf_op jit(solution)/shard_map/ppermute | solution.py:17
  38.6 12.7 %convolution_convert_fusion = bf16[128,2048]{1,0:T(8,128)(2,1)} fusion(bf16[2048,4096]{1,0:T(8,128)(2,1)} %param.15, bf16[128,4096]{1,0:T(8,128)(2,1)} %param.16, pred[128]{0:T(512)(128)(4,1)S(1)} %broadcast_compare_fusion.2), kind=kOutput, calls=%fused_computation.53 | convolution fusion | flops 2148270080 | bytes 18350208 | tf_op jit(solution)/shard_map/dot_general | solution.py:117
  51.4 19.7 %collective-permute-done.1 = bf16[512,512]{0,1:T(8,128)(2,1)S(1)} collective-permute-done((bf16[512,512]{0,1:T(8,128)(2,1)S(1)}, bf16[512,512]{0,1:T(8,128)(2,1)S(1)}, u32[]{:S(2)}, u32[]{:S(2)}) %collective-permute-start.1) | collective-permute-done | bytes 524320 | tf_op jit(solution)/shard_map/ppermute | solution.py:17
  71.7 18.9 %all-gather = bf16[4,1,512]{2,1,0:T(2,128)(2,1)S(1)} all-gather(bf16[1,1,512]{2,1,0:T(2,128)(2,1)S(1)} %reshape.205), channel_id=1, replica_groups=mesh['groups'=2,'ctx'=4,'head'=2,'rep'=2] {'ctx'}, dimensions={0}, use_global_device_ids=true | all-gather | bytes 5120 | tf_op jit(solution)/shard_map/all_gather | solution.py:145
  90.7 1.4 reshape.203
  95.2 54.8 %while.39 = (s32[]{:T(128)}, f32[4,512]{1,0:T(4,128)S(1)}, f32[4,512]{1,0:T(4,128)S(1)}, f32[4,512,128]{2,1,0:T(8,128)}, f32[4,512]{1,0:T(4,128)S(1)}, /*index=5...) while((s32[]{:T(128)}, f32[4,512]{1,0:T(4,128)S(1)}, ...), condition=%wide.region_6.7_spmd.clone, body=%wide.region_1.6_spmd.clone.sunk | while | flops 832591872 | bytes 61090668 | solution.py:92
  95.9 3.4 %fusion.81 = (f32[4,512]{1,0:T(4,128)S(1)}, f32[4,512]{1,0:T(4,128)S(1)}, f32[4,512,512]{2,1,0:T(8,128)}) fusion(pred[512,512]{0,1:T(8,128)(4,1)S(1)} %get-tuple-element.631, pred[512,512]{0,1:T(8,128)(4,1)S(1)} %get-tuple-element.632, bf16[512,4,128]{0,2,1:T(8,128)(2,1)S(1)} %bitcast.121, bf16[4,512,128]{2,1,0:T(8,128)(2,1)S(1)} %get-tuple-element.682), kind=kOutput, calls=%fused_computation.19.clone.1 | convolution fusion | flops 273674240 | bytes 5783552 | tf_op jit(solution)/shard_map/while/body/eval_jaxpr/gqd,tgd->gqt/dot_general | solution.py:28
  99.3 3.7 %fusion.82 = (f32[4,512]{1,0:T(4,128)S(1)}, f32[4,512]{1,0:T(4,128)S(1)}) fusion(f32[4,512,512]{2,1,0:T(8,128)} %get-tuple-element.634, f32[4,512]{1,0:T(4,128)S(1)} %select_maximum_fusion.5, pred[512,512]{0,1:T(8,128)(4,1)S(1)} %get-tuple-element.631, f32[4,512]{1,0:T(4,128)S(1)} %select_maximum_fusion.4, pred[512,512]{0,1:T(8,128)(4,1)S(1)} %get-tuple-element.632), kind=kLoop, calls=%fused_computation.23.clone.1 | loop fusion | flops 9433088 | bytes 4751360 | tf_op jit(solution)/shard_map/while/body/eval_jaxpr/reduce_sum | solution.py:45
  103.1 1.1 constant_dynamic-slice_fusion.10
  104.2 1.9 fusion.85
  106.1 1.9 fusion.84
  108.1 1.0 copy-done.5
  109.6 3.4 %fusion.81 = (f32[4,512]{1,0:T(4,128)S(1)}, f32[4,512]{1,0:T(4,128)S(1)}, f32[4,512,512]{2,1,0:T(8,128)}) fusion(pred[512,512]{0,1:T(8,128)(4,1)S(1)} %get-tuple-element.631, pred[512,512]{0,1:T(8,128)(4,1)S(1)} %get-tuple-element.632, bf16[512,4,128]{0,2,1:T(8,128)(2,1)S(1)} %bitcast.121, bf16[4,512,128]{2,1,0:T(8,128)(2,1)S(1)} %get-tuple-element.682), kind=kOutput, calls=%fused_computation.19.clone.1 | convolution fusion | flops 273674240 | bytes 5783552 | tf_op jit(solution)/shard_map/while/body/eval_jaxpr/gqd,tgd->gqt/dot_general | solution.py:28
  113.0 3.7 %fusion.82 = (f32[4,512]{1,0:T(4,128)S(1)}, f32[4,512]{1,0:T(4,128)S(1)}) fusion(f32[4,512,512]{2,1,0:T(8,128)} %get-tuple-element.634, f32[4,512]{1,0:T(4,128)S(1)} %select_maximum_fusion.5, pred[512,512]{0,1:T(8,128)(4,1)S(1)} %get-tuple-element.631, f32[4,512]{1,0:T(4,128)S(1)} %select_maximum_fusion.4, pred[512,512]{0,1:T(8,128)(4,1)S(1)} %get-tuple-element.632), kind=kLoop, calls=%fused_computation.23.clone.1 | loop fusion | flops 9433088 | bytes 4751360 | tf_op jit(solution)/shard_map/while/body/eval_jaxpr/reduce_sum | solution.py:45
  116.7 1.1 constant_dynamic-slice_fusion.10
  117.8 1.9 fusion.85
  119.8 1.9 fusion.84
  121.7 1.0 copy-done.5
  123.2 3.4 %fusion.81 = (f32[4,512]{1,0:T(4,128)S(1)}, f32[4,512]{1,0:T(4,128)S(1)}, f32[4,512,512]{2,1,0:T(8,128)}) fusion(pred[512,512]{0,1:T(8,128)(4,1)S(1)} %get-tuple-element.631, pred[512,512]{0,1:T(8,128)(4,1)S(1)} %get-tuple-element.632, bf16[512,4,128]{0,2,1:T(8,128)(2,1)S(1)} %bitcast.121, bf16[4,512,128]{2,1,0:T(8,128)(2,1)S(1)} %get-tuple-element.682), kind=kOutput, calls=%fused_computation.19.clone.1 | convolution fusion | flops 273674240 | bytes 5783552 | tf_op jit(solution)/shard_map/while/body/eval_jaxpr/gqd,tgd->gqt/dot_general | solution.py:28
  126.6 3.7 %fusion.82 = (f32[4,512]{1,0:T(4,128)S(1)}, f32[4,512]{1,0:T(4,128)S(1)}) fusion(f32[4,512,512]{2,1,0:T(8,128)} %get-tuple-element.634, f32[4,512]{1,0:T(4,128)S(1)} %select_maximum_fusion.5, pred[512,512]{0,1:T(8,128)(4,1)S(1)} %get-tuple-element.631, f32[4,512]{1,0:T(4,128)S(1)} %select_maximum_fusion.4, pred[512,512]{0,1:T(8,128)(4,1)S(1)} %get-tuple-element.632), kind=kLoop, calls=%fused_computation.23.clone.1 | loop fusion | flops 9433088 | bytes 4751360 | tf_op jit(solution)/shard_map/while/body/eval_jaxpr/reduce_sum | solution.py:45
  130.4 1.1 constant_dynamic-slice_fusion.10
  131.5 1.9 fusion.85
  133.4 1.9 fusion.84
  135.4 1.0 copy-done.5
  136.9 3.4 %fusion.81 = (f32[4,512]{1,0:T(4,128)S(1)}, f32[4,512]{1,0:T(4,128)S(1)}, f32[4,512,512]{2,1,0:T(8,128)}) fusion(pred[512,512]{0,1:T(8,128)(4,1)S(1)} %get-tuple-element.631, pred[512,512]{0,1:T(8,128)(4,1)S(1)} %get-tuple-element.632, bf16[512,4,128]{0,2,1:T(8,128)(2,1)S(1)} %bitcast.121, bf16[4,512,128]{2,1,0:T(8,128)(2,1)S(1)} %get-tuple-element.682), kind=kOutput, calls=%fused_computation.19.clone.1 | convolution fusion | flops 273674240 | bytes 5783552 | tf_op jit(solution)/shard_map/while/body/eval_jaxpr/gqd,tgd->gqt/dot_general | solution.py:28
  140.3 3.7 %fusion.82 = (f32[4,512]{1,0:T(4,128)S(1)}, f32[4,512]{1,0:T(4,128)S(1)}) fusion(f32[4,512,512]{2,1,0:T(8,128)} %get-tuple-element.634, f32[4,512]{1,0:T(4,128)S(1)} %select_maximum_fusion.5, pred[512,512]{0,1:T(8,128)(4,1)S(1)} %get-tuple-element.631, f32[4,512]{1,0:T(4,128)S(1)} %select_maximum_fusion.4, pred[512,512]{0,1:T(8,128)(4,1)S(1)} %get-tuple-element.632), kind=kLoop, calls=%fused_computation.23.clone.1 | loop fusion | flops 9433088 | bytes 4751360 | tf_op jit(solution)/shard_map/while/body/eval_jaxpr/reduce_sum | solution.py:45
  144.0 1.1 constant_dynamic-slice_fusion.10
  145.1 1.9 fusion.85
  147.1 1.9 fusion.84
  150.1 2.4 %multiply_reduce_fusion = (f32[4,512]{1,0:T(4,128)S(1)}, bf16[4,512,128]{2,1,0:T(8,128)(2,1)S(1)}) fusion(f32[4,512,128]{2,1,0:T(8,128)} %get-tuple-element.362, f32[4,512]{1,0:T(4,128)S(1)} %get-tuple-element.363, bf16[4,4,128,128]{3,2,1,0:T(8,128)(2,1)} %copy.73, f32[4,512,128]{2,1,0:T(8,128)} %get-tuple-element.360, f32[4,512]{1,0:T(4,128)S(1)} %get-tuple-element.361), kind=kLoop, calls=%fused_computation.55 | loop fusion | flops 1832960 | bytes 3170304 | tf_op jit(solution)/shard_map/reduce_sum | solution.py:151
  152.7 9.5 %fusion.39 = f32[128,4096]{1,0:T(8,128)} fusion(bf16[128,2048]{0,1:T(8,128)(2,1)S(1)} %bitcast.122, bf16[2048,4096]{1,0:T(8,128)(2,1)} %param.15), kind=kOutput, calls=%fused_computation.79 | convolution fusion | flops 2147483648 | bytes 19398656 | tf_op jit(solution)/shard_map/dot_general | solution.py:178
  162.4 18.1 %while.38 = (s32[]{:T(128)}, f32[2048]{0:T(1024)S(1)}, bf16[2048,512]{0,1:T(8,128)(2,1)}, bf16[4,512,128]{2,1,0:T(8,128)(2,1)S(1)}, f32[4,512]{1,0:T(4,128)S(1)}...) while((s32[]{:T(128)}, f32[2048]{0:T(1024)S(1)}, ...), condition=%wide.region_11.12_spmd.clone, body=%wide.region_9.11_spmd.clone.sunk | while | flops 546570752 | bytes 13140663 | solution.py:92
  162.4 1.3 constant_dynamic-slice_fusion.8
  164.6 2.1 fusion.74
  166.9 1.3 constant_dynamic-slice_fusion.8
  169.1 2.1 fusion.74
  171.4 1.3 constant_dynamic-slice_fusion.8
  173.6 2.1 fusion.74
  175.9 1.3 constant_dynamic-slice_fusion.8
  178.2 2.1 fusion.74
  180.5 11.5 %all-reduce = f32[2048]{0:T(1024)S(1)} all-reduce(f32[2048]{0:T(1024)S(1)} %get-tuple-element.365), channel_id=3, replica_groups=mesh['groups'=2,'ctx'=4,'head'=2,'rep'=2] {'ctx'}, use_global_device_ids=true, to_apply=%region_12.13.clone | all-reduce | flops 2048 | bytes 16384
  192.0 5.6 %psum.14 = f32[512]{0:T(512)S(1)} all-reduce(f32[512]{0:T(512)S(1)} %dynamic-slice.1), channel_id=1, replica_groups=mesh['groups'=2,'ctx'=4,'head'=2,'rep'=2] {'head','rep'}, use_global_device_ids=true, to_apply=%region_13.14 | all-reduce | flops 512 | bytes 4096 | tf_op jit(solution)/shard_map/psum | solution.py:182
  198.0 9.1 %psum.15 = f32[32]{0:T(128)} all-reduce(f32[32]{0:T(128)S(1)} %convolution_bitcast_fusion), channel_id=1, replica_groups=mesh['groups'=2,'ctx'=4,'head'=2,'rep'=2] {'ctx'}, use_global_device_ids=true, to_apply=%region_14.15 | all-reduce | flops 32 | bytes 256 | tf_op jit(solution)/shard_map/psum | solution.py:186
  207.0 2.1 convert_element_type.44
  (155 shorter events, 12.0 us)
Async XLA Ops:
  7.2 88.1 %all-gather.4.cloned.1.call-start = ((), (), s32[]{:S(2)}) async-start(), calls=%async_computation.1 | async-start | bytes 2621440 | tf_op jit(solution)/shard_map/all_gather | solution.py:144
  9.3 153.1 %all-gather.6.cloned.1.call-start = ((), (), s32[]{:S(2)}) async-start(), calls=%async_computation.3 | async-start | bytes 2621440 | tf_op jit(solution)/shard_map/all_gather | solution.py:165
  10.6 5.1 %copy-start.1 = (bf16[512,512]{0,1:T(8,128)(2,1)}, bf16[512,512]{0,1:T(8,128)(2,1)S(1)}, u32[]{:S(2)}) copy-start(bf16[512,512]{0,1:T(8,128)(2,1)S(1)} %copy.67) | copy-start | bytes 1572868
  10.6 23.7 %collective-permute-start = (bf16[512,512]{0,1:T(8,128)(2,1)S(1)}, bf16[512,512]{0,1:T(8,128)(2,1)S(1)}, u32[]{:S(2)}, u32[]{:S(2)}) collective-permute-start(bf16[512,512]{0,1:T(8,128)(2,1)S(1)} %copy.67), channel_id=1, source_target_pairs={{0,12},{4,0},{8,4},{12,8},{1,13},{5,1},{9,5},{13,9},{2,14},{6,2},{... | collective-permute-start | bytes 1572872 | tf_op jit(solution)/shard_map/ppermute | solution.py:17
  15.7 191.3 %reduce-scatter.2.cloned.1.call-start = ((), (), s32[]{:S(2)}) async-start(), calls=%async_computation.2 | async-start | bytes 3145728 | tf_op jit(solution)/shard_map/reduce_scatter | solution.py:179
  16.4 34.8 %copy-start.9 = (s32[512]{0:T(512)S(1)}, s32[512]{0:T(512)}, u32[]{:S(2)}) copy-start(s32[512]{0:T(512)} %param.18) | copy-start | bytes 6148
  16.4 34.8 %copy-start.11 = (s32[4]{0:T(128)S(1)}, s32[4]{0:T(128)}, u32[]{:S(2)}) copy-start(s32[4]{0:T(128)} %param.19) | copy-start | bytes 52
  34.3 36.9 %copy-start.8 = (bf16[128,2048]{1,0:T(8,128)(2,1)S(1)}, bf16[128,2048]{1,0:T(8,128)(2,1)}, u32[]{:S(2)}) copy-start(bf16[128,2048]{1,0:T(8,128)(2,1)} %param.12) | copy-start | bytes 1572868
  34.3 36.8 %collective-permute-start.1 = (bf16[512,512]{0,1:T(8,128)(2,1)S(1)}, bf16[512,512]{0,1:T(8,128)(2,1)S(1)}, u32[]{:S(2)}, u32[]{:S(2)}) collective-permute-start(bf16[512,512]{0,1:T(8,128)(2,1)S(1)} %collective-permute-done), channel_id=1, source_target_pairs={{0,12},{4,0},{8,4},{12,8},{1,13},{5,1},{9,5},{13,9},{2,14},{6,2},{... | collective-permute-start | bytes 1572872 | tf_op jit(solution)/shard_map/ppermute | solution.py:17
  51.3 41.8 %copy-start.12 = (u32[32]{0:T(128)S(1)}, u32[32]{0:T(128)}, u32[]{:S(2)}) copy-start(u32[32]{0:T(128)} %constant.154) | copy-start | bytes 388
  51.3 43.1 %copy-start.2 = (bf16[512,512]{0,1:T(8,128)(2,1)S(1)}, bf16[512,512]{0,1:T(8,128)(2,1)}, u32[]{:S(2)}) copy-start(bf16[512,512]{0,1:T(8,128)(2,1)} %copy-done.1) | copy-start | bytes 1572868
  71.1 23.6 %collective-permute-start.2 = (bf16[512,512]{0,1:T(8,128)(2,1)S(1)}, bf16[512,512]{0,1:T(8,128)(2,1)S(1)}, u32[]{:S(2)}, u32[]{:S(2)}) collective-permute-start(bf16[512,512]{0,1:T(8,128)(2,1)S(1)} %collective-permute-done.1), channel_id=1, source_target_pairs={{0,12},{4,0},{8,4},{12,8},{1,13},{5,1},{9,5},{13,9},{2,14},{6,2},{... | collective-permute-start | bytes 1572872 | tf_op jit(solution)/shard_map/ppermute | solution.py:17
  99.3 4.9 %copy-start = (f32[4,512,512]{2,1,0:T(8,128)S(1)}, f32[4,512,512]{2,1,0:T(8,128)}, u32[]{:S(2)}) copy-start(f32[4,512,512]{2,1,0:T(8,128)} %get-tuple-element.634) | copy-start | bytes 12582916 | tf_op jit(solution)/shard_map/while
  99.3 4.9 %copy-start.6 = (f32[4,512,128]{2,1,0:T(8,128)S(1)}, f32[4,512,128]{2,1,0:T(8,128)}, u32[]{:S(2)}) copy-start(f32[4,512,128]{2,1,0:T(8,128)} %get-tuple-element.664) | copy-start | bytes 3145732 | tf_op jit(solution)/shard_map/while
  104.2 1.9 copy-start.4
  106.1 1.9 copy-start.7
  108.0 1.1 copy-start.5
  112.9 4.9 %copy-start = (f32[4,512,512]{2,1,0:T(8,128)S(1)}, f32[4,512,512]{2,1,0:T(8,128)}, u32[]{:S(2)}) copy-start(f32[4,512,512]{2,1,0:T(8,128)} %get-tuple-element.634) | copy-start | bytes 12582916 | tf_op jit(solution)/shard_map/while
  113.0 4.9 %copy-start.6 = (f32[4,512,128]{2,1,0:T(8,128)S(1)}, f32[4,512,128]{2,1,0:T(8,128)}, u32[]{:S(2)}) copy-start(f32[4,512,128]{2,1,0:T(8,128)} %get-tuple-element.664) | copy-start | bytes 3145732 | tf_op jit(solution)/shard_map/while
  117.8 1.9 copy-start.4
  119.8 1.9 copy-start.7
  121.7 1.1 copy-start.5
  126.6 4.9 %copy-start = (f32[4,512,512]{2,1,0:T(8,128)S(1)}, f32[4,512,512]{2,1,0:T(8,128)}, u32[]{:S(2)}) copy-start(f32[4,512,512]{2,1,0:T(8,128)} %get-tuple-element.634) | copy-start | bytes 12582916 | tf_op jit(solution)/shard_map/while
  126.6 4.9 %copy-start.6 = (f32[4,512,128]{2,1,0:T(8,128)S(1)}, f32[4,512,128]{2,1,0:T(8,128)}, u32[]{:S(2)}) copy-start(f32[4,512,128]{2,1,0:T(8,128)} %get-tuple-element.664) | copy-start | bytes 3145732 | tf_op jit(solution)/shard_map/while
  131.5 1.9 copy-start.4
  133.4 1.9 copy-start.7
  135.4 1.1 copy-start.5
  140.3 4.9 %copy-start = (f32[4,512,512]{2,1,0:T(8,128)S(1)}, f32[4,512,512]{2,1,0:T(8,128)}, u32[]{:S(2)}) copy-start(f32[4,512,512]{2,1,0:T(8,128)} %get-tuple-element.634) | copy-start | bytes 12582916 | tf_op jit(solution)/shard_map/while
  140.3 4.9 %copy-start.6 = (f32[4,512,128]{2,1,0:T(8,128)S(1)}, f32[4,512,128]{2,1,0:T(8,128)}, u32[]{:S(2)}) copy-start(f32[4,512,128]{2,1,0:T(8,128)} %get-tuple-element.664) | copy-start | bytes 3145732 | tf_op jit(solution)/shard_map/while
  145.1 1.9 copy-start.4
  147.1 1.9 copy-start.7
  149.0 1.1 copy-start.5
  152.7 9.6 %copy-start.3 = (bf16[4,4,128,128]{3,2,1,0:T(8,128)(2,1)S(1)}, bf16[4,4,128,128]{3,2,1,0:T(8,128)(2,1)}, u32[]{:S(2)}) copy-start(bf16[4,4,128,128]{3,2,1,0:T(8,128)(2,1)} %copy.73) | copy-start | bytes 1572868
  197.7 11.4 %copy-start.10 = (f32[512]{0:T(512)}, f32[512]{0:T(512)S(1)}, u32[]{:S(2)}) copy-start(f32[512]{0:T(512)S(1)} %psum.14) | copy-start | bytes 6148
Sparse Core Ops, SparseCore 0:
  9.6 65.5 all-gather.3
  77.3 48.8 all-gather.5
  162.4 32.3 reduce-scatter.1
